TPU v7x, 32 devices: a whole 2x2x4 slice. The times are simulated.
32 devices in a mesh: blk: 8 (over z, y), harvest: 4 (over x, core).
Axes of the slice: x: 2, y: 2, z: 4, core: 2. Of those that a mesh axis runs over, the one named last changes fastest.
Arguments:
- grad_rows: bfloat16 [8192, 8192], P(('blk', 'harvest')), may hold values from -1500 to 1500
- row_weights: float32 [8192], P(('blk', 'harvest')), may hold values from 0.25 to 4
- destinations: int32 [8192, 1], P(('blk', 'harvest')), may hold values from 0 to 7; in each aligned block of 256 rows (0 to 255, 256 to 511, ...) at most 48 rows name the same one
- queries: bfloat16 [128, 8192], P(('blk', 'harvest')), may hold values from -6 to 6
- tile_pattern: int32 [8, 8], replicated, may hold values from 0 to 1, as said below
Outputs:
- scores: bfloat16 [12288, 128], P(('blk', 'harvest'))
Inputs may be any that keep to these rules, and one draw needn't show every extreme that they name: `destinations`: in the rows of one device no owner is named more than 48 times, a bound that some block reaches. tile_pattern[a, b] is 1 where the tile of query block a and owner b is scored.
All inputs are finite; a program needn't handle non-finite values.
Results may differ from a plain program's by a relative error of at most 0.0095.
Values may be sent and summed in bfloat16 or wider, within the bound.
No kernel may reach another device: no remote copies, remote signals or barrier semaphores. Data moves between devices by JAX's collectives and lax.ppermute only.
A program may use at most 128 MiB of HBM per device.

v0:
```python
import math
import jax
import jax.numpy as jnp
from jax import lax
from jax.sharding import PartitionSpec as P


def make_tile(left_rows, weight_scale, shard_rows, tile_mask):
    product = jnp.einsum("sk,pk->sp", left_rows, shard_rows, preferred_element_type=jnp.float32)
    return product * weight_scale[:, None] * tile_mask


def circulate(prepared, folding, initial):
    block_queries = lax.all_gather(prepared, "harvest", axis=0, tiled=True)
    return folding(initial, lax.all_gather(block_queries, "blk", axis=0, tiled=True), jnp.int32(0))


def local(grad_rows, row_weights, destinations, queries, tile_pattern):
    blk_count = lax.axis_size("blk")
    harv_count = lax.axis_size("harvest")
    row_count = grad_rows.shape[0]
    width = grad_rows.shape[1]
    capacity = max(3 * row_count // (2 * blk_count), 2)
    block_size = queries.shape[0] * harv_count
    query_count = block_size * blk_count
    inv_root = 1.0 / math.sqrt(width)
    squares = jnp.sum(row_weights[:, None] * jnp.square(grad_rows.astype(jnp.float32)), axis=0)
    total_sq, total_weight = lax.psum((squares, jnp.sum(row_weights)), ("blk", "harvest"))
    scaling = lax.rsqrt(total_sq / total_weight + 1e-06)
    prepared = (queries.astype(jnp.float32) * scaling).astype(jnp.bfloat16)
    owner_ids = destinations[:, 0]
    one_hot = (owner_ids[:, None] == jnp.arange(blk_count, dtype=jnp.int32)[None, :]).astype(
        jnp.int32
    )
    before = jnp.cumsum(one_hot, axis=0) - one_hot
    slot_rank = jnp.sum(before * one_hot, axis=1)
    slot_index = owner_ids * capacity + slot_rank
    weight_scale = row_weights * inv_root
    slot_total = blk_count * capacity
    bucket_rows = jnp.zeros((slot_total, width), jnp.bfloat16).at[slot_index].set(grad_rows)
    bucket_weights = jnp.zeros((slot_total,), jnp.float32).at[slot_index].set(weight_scale)
    slot_rows, slot_weights = (
        lax.all_to_all(
            bucket_rows.reshape(blk_count, capacity, width),
            "blk",
            split_axis=0,
            concat_axis=0,
            tiled=True,
        ),
        lax.all_to_all(
            bucket_weights.reshape(blk_count, capacity).astype(jnp.bfloat16),
            "blk",
            split_axis=0,
            concat_axis=0,
            tiled=True,
        ).astype(jnp.float32),
    )
    slot_rows = slot_rows.reshape(slot_total, width)
    slot_weights = slot_weights.reshape(slot_total)
    owner_index = lax.axis_index("blk")
    pattern_column = lax.dynamic_slice(tile_pattern, (0, owner_index), (blk_count, 1))[:, 0]
    query_mask = jnp.repeat(pattern_column.astype(jnp.float32), block_size)

    def fold_owner(running, shard_rows, offset):
        tile_mask = query_mask[None, :]
        tile_values = make_tile(slot_rows, slot_weights, shard_rows, tile_mask)
        return lax.dynamic_update_slice_in_dim(running, tile_values, offset, 1)

    initial = jnp.zeros((slot_total, query_count), jnp.float32)
    return circulate(prepared, fold_owner, initial).astype(jnp.bfloat16)


def solution(mesh):
    in_specs = (
        P(("blk", "harvest"), None),
        P(("blk", "harvest")),
        P(("blk", "harvest"), None),
        P(("blk", "harvest"), None),
        P(),
    )
    out_specs = P(("blk", "harvest"), None)
    return jax.shard_map(local, mesh=mesh, in_specs=in_specs, out_specs=out_specs, check_vma=False)
```

profile of v0, /device:TPU:0, one launch (start us, length us, event | category | flops | bytes accessed | tf_op | source)
XLA Modules:
  0.0 264.9 jit_solution(10223305340122949333)
XLA Ops:
  6.5 0.7 fusion.7
  7.2 0.6 reduce-window.6
  7.8 0.2 slice_reduce_fusion
  8.0 0.8 fusion.6
  8.8 0.7 compare_select_fusion
  9.5 1.3 broadcast_multiply_fusion
  10.8 1.4 scatter_custom_fusion.1
  12.2 0.7 convert_element_type.61
  12.9 7.3 %all-to-all-start.1 = ((bf16[8,1,48]{2,1,0:T(2,128)(2,1)}), bf16[8,1,48]{2,1,0:T(2,128)(2,1)S(1)}, u32[]{:S(2)}, u32[]{:S(2)}) async-start(bf16[8,1,48]{2,1,0:T(2,128)(2,1)} %convert_element_type.61), calls=%async_computation.1 | async-start | bytes 8192 | tf_op jit(solution)/shard_map/all_to_all | solution.py:50
  20.2 11.3 %scatter_custom_fusion = bf16[384,8192]{1,0:T(8,128)(2,1)} fusion(s32[256]{0:T(256)S(1)} %bitcast.23, bf16[256,8192]{1,0:T(8,128)(2,1)} %param.5, bf16[]{:T(256)} %constant.10.clone.1), kind=kCustom, calls=%fused_computation.3 | custom fusion | bytes 6291968 | tf_op jit(solution)/shard_map/scatter | solution.py:40
  31.4 0.0 all-to-all-done.1
  31.5 0.0 copy-start.1
  31.5 0.0 copy-start
  31.5 0.0 copy-start.2
  31.5 6.1 %all-to-all-start = ((bf16[8,48,8192]{2,1,0:T(8,128)(2,1)}), bf16[8,48,8192]{2,1,0:T(8,128)(2,1)}, u32[]{:S(2)}, u32[]{:S(2)}) async-start(bf16[8,48,8192]{2,1,0:T(8,128)(2,1)} %bitcast.18), calls=%async_computation | async-start | bytes 12582912 | tf_op jit(solution)/shard_map/all_to_all | solution.py:43
  37.6 0.0 all-gather.3.cloned.1.call-start
  37.7 0.0 copy-done.1
  37.7 3.3 %multiply_reduce_fusion = f32[8192]{0:T(1024)S(1)} fusion(bf16[256,8192]{1,0:T(8,128)(2,1)} %param.5, f32[256]{0:T(256)S(1)} %copy-done.1), kind=kLoop, calls=%fused_computation.2 | loop fusion | flops 8380416 | bytes 4228096 | tf_op jit(solution)/shard_map/reduce_sum | solution.py:27
  41.0 154.6 %all-reduce = (f32[8192]{0:T(1024)S(1)}, f32[]{:T(128)}) all-reduce(f32[8192]{0:T(1024)S(1)} %multiply_reduce_fusion, f32[]{:T(128)} %get-tuple-element.8), channel_id=1, replica_groups=mesh['blk'=8,'harvest'=4] {'blk','harvest'}, use_global_device_ids=true, to_apply=%region_5.6 | all-reduce | flops 8193 | bytes 65544 | tf_op jit(solution)/shard_map/psum | solution.py:28
  195.6 0.7 add_rsqrt_fusion
  196.3 0.0 copy-done
  196.3 6.5 %all-gather = bf16[4,4,8192]{2,1,0:T(4,128)(2,1)S(1)} all-gather(bf16[1,4,8192]{2,1,0:T(4,128)(2,1)S(1)} %fusion.4), channel_id=1, replica_groups=mesh['blk'=8,'harvest'=4] {'harvest'}, dimensions={0}, use_global_device_ids=true | all-gather | bytes 327680 | tf_op jit(solution)/shard_map/all_gather | solution.py:14
  202.9 0.8 reshape.69
  203.6 0.0 all-gather.3.cloned.1.call-update
  203.7 0.0 copy-done.2
  203.7 0.2 convert_reduce_fusion.1
  203.9 0.1 broadcast_in_dim.16
  203.9 0.1 mul.61
  204.1 0.1 reshape.51
  204.1 48.1 %all-gather.3.cloned.1.call-done = bf16[128,8192]{1,0:T(8,128)(2,1)} async-done(((bf16[16,8192]{1,0:T(8,128)(2,1)}), bf16[128,8192]{1,0:T(8,128)(2,1)}) %all-gather.3.cloned.1.call-update) | async-done | bytes 2097168 | tf_op jit(solution)/shard_map/all_gather | solution.py:15
  252.2 0.0 all-to-all-done
  252.2 5.8 %fusion.3 = bf16[384,128]{1,0:T(8,128)(2,1)} fusion(bf16[384,8192]{1,0:T(8,128)(2,1)} %bitcast.7, bf16[128,8192]{1,0:T(8,128)(2,1)} %all-gather.3.cloned.1.call-done, f32[128]{0:T(128)S(1)} %mul.61, f32[384]{0:T(512)S(1)} %reshape.51), kind=kOutput, calls=%fused_computation.7 | convolution fusion | flops 805453824 | bytes 8488960 | tf_op jit(solution)/shard_map/sk,pk->sp/dot_general | solution.py:9
  (5 shorter events, 0.1 us)
Async XLA Ops:
  12.9 18.5 %all-to-all-start.1 = ((bf16[8,1,48]{2,1,0:T(2,128)(2,1)}), bf16[8,1,48]{2,1,0:T(2,128)(2,1)S(1)}, u32[]{:S(2)}, u32[]{:S(2)}) async-start(bf16[8,1,48]{2,1,0:T(2,128)(2,1)} %convert_element_type.61), calls=%async_computation.1 | async-start | bytes 8192 | tf_op jit(solution)/shard_map/all_to_all | solution.py:50
  31.5 6.2 %copy-start.1 = (f32[256]{0:T(256)S(1)}, f32[256]{0:T(256)}, u32[]{:S(2)}) copy-start(f32[256]{0:T(256)} %param.6) | copy-start | bytes 3076
  31.5 164.8 %copy-start = (bf16[4,8192]{1,0:T(4,128)(2,1)S(1)}, bf16[4,8192]{1,0:T(4,128)(2,1)}, u32[]{:S(2)}) copy-start(bf16[4,8192]{1,0:T(4,128)(2,1)} %param.8) | copy-start | bytes 196612
  31.5 172.2 %copy-start.2 = (s32[8,8]{1,0:T(8,128)S(1)}, s32[8,8]{1,0:T(8,128)}, u32[]{:S(2)}) copy-start(s32[8,8]{1,0:T(8,128)} %param.9) | copy-start | bytes 772
  31.5 220.7 %all-to-all-start = ((bf16[8,48,8192]{2,1,0:T(8,128)(2,1)}), bf16[8,48,8192]{2,1,0:T(8,128)(2,1)}, u32[]{:S(2)}, u32[]{:S(2)}) async-start(bf16[8,48,8192]{2,1,0:T(8,128)(2,1)} %bitcast.18), calls=%async_computation | async-start | bytes 12582912 | tf_op jit(solution)/shard_map/all_to_all | solution.py:43
  37.6 214.6 %all-gather.3.cloned.1.call-start = ((), (), s32[]{:S(2)}) async-start(), calls=%async_computation.2 | async-start | bytes 2359296 | tf_op jit(solution)/shard_map/all_gather | solution.py:15
Sparse Core Ops, SparseCore 0:
  203.8 48.3 all-gather.2
where the time goes:
time: 265 us
  blocking collectives  161 us (61%)
  waiting for transfers between devices  48.1 us (18%)
  local copies, waits for them, and re-layouts  14.6 us (6%)
  starting transfers between devices  13.5 us (5%)
  between operations  13.5 us (5%)
  other arithmetic  8.31 us (3%)
  matrix products  5.85 us (2%)
    psum x1, blocking collectives, local(): lax.psum((squares, jnp.sum(row_weights)), ('blk', 'harvest'))  155 us
    all_gather x1, waiting for transfers between devices, circulate(): lax.all_gather(block_queries, 'blk', axis=0, tiled=True)  48.1 us
    scatter x1, local copies, waits for them, and re-layouts, local(): jnp.zeros((slot_total, width), jnp.bfloat16).at[slot_index].set(grad_rows)  11.3 us
    all_to_all x1, starting transfers between devices, local(): lax.all_to_all(bucket_weights.reshape(blk_count, capacity).astype(jnp.bfl...  7.28 us
    all_gather x1, blocking collectives, circulate(): block_queries = lax.all_gather(prepared, 'harvest', axis=0, tiled=True)  6.53 us
    all_to_all x1, starting transfers between devices, local(): lax.all_to_all(bucket_rows.reshape(blk_count, capacity, width), 'blk', sp...  6.14 us
    dot_general x1, matrix products, make_tile(): jnp.einsum('sk,pk->sp', left_rows, shard_rows, preferred_element_type=jnp...  5.85 us
  transfers between devices with their start and end apart: 3, of which 1 were waited for; matrix products, arithmetic and copies ran while one was open for 6% of the time, Pallas kernels for 0%

commit v1 on v0

--- a/solution.py
+++ b/solution.py
@@ -3,6 +3,22 @@
 import jax.numpy as jnp
 from jax import lax
 from jax.sharding import PartitionSpec as P
+
+
+def swapped_with_each(x, axis, split, join):
+    ways, here = (lax.axis_size(axis), lax.axis_index(axis))
+    width = x.shape[split] // ways
+    dims = list(x.shape)
+    dims[split] = width
+    height = dims[join]
+    dims[join] = height * ways
+    full = jnp.zeros(dims, x.dtype)
+    for mask in range(ways):
+        part = lax.dynamic_slice_in_dim(x, (here ^ mask) * width, width, axis=split)
+        if mask:
+            part = lax.ppermute(part, axis, [(d, d ^ mask) for d in range(ways)])
+        full = lax.dynamic_update_slice_in_dim(full, part, (here ^ mask) * height, axis=join)
+    return full
 
 
 def make_tile(left_rows, weight_scale, shard_rows, tile_mask):
@@ -40,13 +56,7 @@
     bucket_rows = jnp.zeros((slot_total, width), jnp.bfloat16).at[slot_index].set(grad_rows)
     bucket_weights = jnp.zeros((slot_total,), jnp.float32).at[slot_index].set(weight_scale)
     slot_rows, slot_weights = (
-        lax.all_to_all(
-            bucket_rows.reshape(blk_count, capacity, width),
-            "blk",
-            split_axis=0,
-            concat_axis=0,
-            tiled=True,
-        ),
+        swapped_with_each(bucket_rows.reshape(blk_count, capacity, width), "blk", 0, 0),
         lax.all_to_all(
             bucket_weights.reshape(blk_count, capacity).astype(jnp.bfloat16),
             "blk",

time: 265 us -> 242 us (0.913)
  the two profiles are of different devices: /device:TPU:0 before, /device:TPU:8 now
where the time goes in v1:
time: 242 us; the launch traced here: 241 us
  blocking collectives  82.3 us (34%)
  waiting for transfers between devices  82.2 us (34%)
  local copies, waits for them, and re-layouts  34.1 us (14%)
  starting transfers between devices  15.7 us (6%)
  between operations  13.5 us (6%)
  other arithmetic  7.59 us (3%)
  matrix products  5.85 us (2%)
    ppermute x7, waiting for transfers between devices, swapped_with_each(): part = lax.ppermute(part, axis, [(d, d ^ mask) for d in range(ways)])  82.2 us
    psum x1, blocking collectives, local(): lax.psum((squares, jnp.sum(row_weights)), ('blk', 'harvest'))  75.8 us
    dynamic_update_slice x7, local copies, waits for them, and re-layouts, swapped_with_each(): lax.dynamic_update_slice_in_dim(full, part, (here ^ mask) * height, axis=...  12.3 us
    scatter x1, local copies, waits for them, and re-layouts, local(): jnp.zeros((slot_total, width), jnp.bfloat16).at[slot_index].set(grad_rows)  11.3 us
    ppermute x7, starting transfers between devices, swapped_with_each(): part = lax.ppermute(part, axis, [(d, d ^ mask) for d in range(ways)])  10.4 us
    all_gather x1, blocking collectives, circulate(): block_queries = lax.all_gather(prepared, 'harvest', axis=0, tiled=True)  6.53 us
    dot_general x1, matrix products, make_tile(): jnp.einsum('sk,pk->sp', left_rows, shard_rows, preferred_element_type=jnp...  5.85 us
    unnamed x11, local copies, waits for them, and re-layouts  5.48 us
  transfers between devices with their start and end apart: 9, of which 2 were waited for; matrix products, arithmetic and copies ran while one was open for 8% of the time, Pallas kernels for 0%

profile of v1, /device:TPU:8, one launch (start us, length us, event | category | flops | bytes accessed | tf_op | source)
XLA Modules:
  0.0 241.3 jit_solution(9055064896864787328)
XLA Ops:
  6.5 0.7 fusion.7
  7.2 0.6 reduce-window.6
  7.8 0.2 slice_reduce_fusion
  8.0 0.8 fusion.6
  8.8 0.7 compare_select_fusion
  9.5 11.3 %scatter_custom_fusion = bf16[384,8192]{1,0:T(8,128)(2,1)} fusion(s32[256]{0:T(256)S(1)} %bitcast.23, bf16[256,8192]{1,0:T(8,128)(2,1)} %param.5, bf16[]{:T(256)} %constant.17.clone.1), kind=kCustom, calls=%fused_computation.3 | custom fusion | bytes 6291968 | tf_op jit(solution)/shard_map/scatter | solution.py:56
  20.8 0.0 copy-start
  20.8 0.7 broadcast_in_dim.8
  21.5 2.0 copy-done
  23.6 0.0 copy-start.3
  23.6 0.0 copy-start.2
  23.6 0.0 copy-start.4
  23.6 1.7 constant_dynamic-slice_fusion.1
  25.3 0.0 copy-start.1
  25.3 2.7 %copy-done.1 = bf16[8,48,8192]{2,1,0:T(8,128)(2,1)} copy-done((bf16[8,48,8192]{2,1,0:T(8,128)(2,1)}, bf16[8,48,8192]{2,1,0:T(8,128)(2,1)S(1)}, u32[]{:S(2)}) %copy-start.1) | copy-done | bytes 6291480
  28.0 1.5 collective-permute-start
  29.5 0.4 collective-permute-start.1
  29.9 1.5 collective-permute-start.2
  31.4 2.6 %collective-permute-start.3 = (bf16[1,48,8192]{2,1,0:T(8,128)(2,1)S(1)}, bf16[1,48,8192]{2,1,0:T(8,128)(2,1)}, u32[]{:S(2)}, u32[]{:S(2)}) collective-permute-start(bf16[1,48,8192]{2,1,0:T(8,128)(2,1)S(1)} %get-tuple-element.10), channel_id=1, source_target_pairs={{0,16},{4,20},{8,24},{12,28},{16,0},{20,4},{24,8},{28,12},{1,17},{... | collective-permute-start | bytes 2359304 | tf_op jit(solution)/shard_map/ppermute | solution.py:19
  34.0 1.3 collective-permute-start.4
  35.3 0.0 copy-done.3
  35.3 0.6 broadcast_multiply_fusion
  35.9 1.4 scatter_custom_fusion.1
  37.4 0.7 convert_element_type.61
  38.0 5.3 %all-to-all-start = ((bf16[8,1,48]{2,1,0:T(2,128)(2,1)}), bf16[8,1,48]{2,1,0:T(2,128)(2,1)S(1)}, u32[]{:S(2)}, u32[]{:S(2)}) async-start(bf16[8,1,48]{2,1,0:T(2,128)(2,1)} %convert_element_type.61), calls=%async_computation | async-start | bytes 8192 | tf_op jit(solution)/shard_map/all_to_all | solution.py:60
  43.4 0.0 all-gather.3.cloned.1.call-start
  43.4 3.3 %multiply_reduce_fusion = f32[8192]{0:T(1024)S(1)} fusion(bf16[256,8192]{1,0:T(8,128)(2,1)} %param.5, f32[256]{0:T(256)S(1)} %copy-done.3), kind=kLoop, calls=%fused_computation.2 | loop fusion | flops 8380416 | bytes 4228096 | tf_op jit(solution)/shard_map/reduce_sum | solution.py:43
  46.7 75.8 %all-reduce = (f32[8192]{0:T(1024)S(1)}, f32[]{:T(128)}) all-reduce(f32[8192]{0:T(1024)S(1)} %multiply_reduce_fusion, f32[]{:T(128)} %get-tuple-element.16), channel_id=1, replica_groups=mesh['blk'=8,'harvest'=4] {'blk','harvest'}, use_global_device_ids=true, to_apply=%region_5.6 | all-reduce | flops 8193 | bytes 65544 | tf_op jit(solution)/shard_map/psum | solution.py:44
  122.5 0.6 add_rsqrt_fusion
  123.2 0.0 copy-done.2
  123.2 6.5 %all-gather = bf16[4,4,8192]{2,1,0:T(4,128)(2,1)S(1)} all-gather(bf16[1,4,8192]{2,1,0:T(4,128)(2,1)S(1)} %fusion.4), channel_id=1, replica_groups=mesh['blk'=8,'harvest'=4] {'harvest'}, dimensions={0}, use_global_device_ids=true | all-gather | bytes 327680 | tf_op jit(solution)/shard_map/all_gather | solution.py:30
  129.7 0.8 reshape.69
  130.5 0.0 all-gather.3.cloned.1.call-update
  130.5 0.0 copy-done.4
  130.5 0.2 fusion.9
  130.7 0.1 broadcast_in_dim.20
  130.8 0.1 mul.61
  130.9 0.0 all-to-all-done
  130.9 0.1 reshape.51
  131.0 0.0 collective-permute-done
  131.0 0.7 collective-permute-start.5
  131.7 2.1 constant_dynamic-update-slice_fusion.6
  133.7 0.0 collective-permute-done.1
  133.7 2.4 collective-permute-start.6
  136.1 2.1 constant_dynamic-update-slice_fusion.5
  138.2 0.0 collective-permute-done.2
  138.2 2.1 constant_dynamic-update-slice_fusion.4
  140.3 0.0 collective-permute-done.3
  140.3 2.1 constant_dynamic-update-slice_fusion.3
  142.4 0.0 collective-permute-done.4
  142.4 2.1 constant_dynamic-update-slice_fusion.2
  144.5 57.1 %collective-permute-done.5 = bf16[1,48,8192]{2,1,0:T(8,128)(2,1)S(1)} collective-permute-done((bf16[1,48,8192]{2,1,0:T(8,128)(2,1)S(1)}, bf16[1,48,8192]{2,1,0:T(8,128)(2,1)S(1)}, u32[]{:S(2)}, u32[]{:S(2)}) %collective-permute-start.5) | collective-permute-done | bytes 786464 | tf_op jit(solution)/shard_map/ppermute | solution.py:19
  201.6 0.9 constant_dynamic-update-slice_fusion.1
  202.5 25.1 %collective-permute-done.6 = bf16[1,48,8192]{2,1,0:T(8,128)(2,1)S(1)} collective-permute-done((bf16[1,48,8192]{2,1,0:T(8,128)(2,1)S(1)}, bf16[1,48,8192]{2,1,0:T(8,128)(2,1)S(1)}, u32[]{:S(2)}, u32[]{:S(2)}) %collective-permute-start.6) | collective-permute-done | bytes 786464 | tf_op jit(solution)/shard_map/ppermute | solution.py:19
  227.7 0.9 constant_dynamic-update-slice_fusion
  228.6 0.0 all-gather.3.cloned.1.call-done
  228.6 5.8 %fusion.3 = bf16[384,128]{1,0:T(8,128)(2,1)} fusion(bf16[384,8192]{1,0:T(8,128)(2,1)} %bitcast.19, bf16[128,8192]{1,0:T(8,128)(2,1)} %all-gather.3.cloned.1.call-done, f32[128]{0:T(128)S(1)} %mul.61, f32[384]{0:T(512)S(1)} %reshape.51), kind=kOutput, calls=%fused_computation.7 | convolution fusion | flops 805453824 | bytes 8488960 | tf_op jit(solution)/shard_map/sk,pk->sp/dot_general | solution.py:25
  (5 shorter events, 0.1 us)
Async XLA Ops:
  20.8 2.8 %copy-start = (bf16[384,8192]{1,0:T(8,128)(2,1)S(1)}, bf16[384,8192]{1,0:T(8,128)(2,1)}, u32[]{:S(2)}) copy-start(bf16[384,8192]{1,0:T(8,128)(2,1)} %scatter_custom_fusion) | copy-start | bytes 18874372
  23.6 11.8 %copy-start.3 = (f32[256]{0:T(256)S(1)}, f32[256]{0:T(256)}, u32[]{:S(2)}) copy-start(f32[256]{0:T(256)} %param.6) | copy-start | bytes 3076
  23.6 99.6 %copy-start.2 = (bf16[4,8192]{1,0:T(4,128)(2,1)S(1)}, bf16[4,8192]{1,0:T(4,128)(2,1)}, u32[]{:S(2)}) copy-start(bf16[4,8192]{1,0:T(4,128)(2,1)} %param.8) | copy-start | bytes 196612
  23.6 107.0 %copy-start.4 = (s32[8,8]{1,0:T(8,128)S(1)}, s32[8,8]{1,0:T(8,128)}, u32[]{:S(2)}) copy-start(s32[8,8]{1,0:T(8,128)} %param.9) | copy-start | bytes 772
  25.3 2.7 %copy-start.1 = (bf16[8,48,8192]{2,1,0:T(8,128)(2,1)}, bf16[8,48,8192]{2,1,0:T(8,128)(2,1)S(1)}, u32[]{:S(2)}) copy-start(bf16[8,48,8192]{2,1,0:T(8,128)(2,1)S(1)} %get-tuple-element.14) | copy-start | bytes 18874372
  28.0 103.0 %collective-permute-start = (bf16[1,48,8192]{2,1,0:T(8,128)(2,1)}, bf16[1,48,8192]{2,1,0:T(8,128)(2,1)}, u32[]{:S(2)}, u32[]{:S(2)}) collective-permute-start(bf16[1,48,8192]{2,1,0:T(8,128)(2,1)} %get-tuple-element.13), channel_id=1, source_target_pairs={{0,4},{4,0},{8,12},{12,8},{16,20},{20,16},{24,28},{28,24},{1,5},{5... | collective-permute-start | bytes 2359304 | tf_op jit(solution)/shard_map/ppermute | solution.py:19
  29.5 104.3 %collective-permute-start.1 = (bf16[1,48,8192]{2,1,0:T(8,128)(2,1)}, bf16[1,48,8192]{2,1,0:T(8,128)(2,1)}, u32[]{:S(2)}, u32[]{:S(2)}) collective-permute-start(bf16[1,48,8192]{2,1,0:T(8,128)(2,1)} %get-tuple-element.12), channel_id=1, source_target_pairs={{0,8},{4,12},{8,0},{12,4},{16,24},{20,28},{24,16},{28,20},{1,9},{5... | collective-permute-start | bytes 2359304 | tf_op jit(solution)/shard_map/ppermute | solution.py:19
  29.9 108.3 %collective-permute-start.2 = (bf16[1,48,8192]{2,1,0:T(8,128)(2,1)}, bf16[1,48,8192]{2,1,0:T(8,128)(2,1)}, u32[]{:S(2)}, u32[]{:S(2)}) collective-permute-start(bf16[1,48,8192]{2,1,0:T(8,128)(2,1)} %get-tuple-element.11), channel_id=1, source_target_pairs={{0,12},{4,8},{8,4},{12,0},{16,28},{20,24},{24,20},{28,16},{1,13},{... | collective-permute-start | bytes 2359304 | tf_op jit(solution)/shard_map/ppermute | solution.py:19
  31.4 108.9 %collective-permute-start.3 = (bf16[1,48,8192]{2,1,0:T(8,128)(2,1)S(1)}, bf16[1,48,8192]{2,1,0:T(8,128)(2,1)}, u32[]{:S(2)}, u32[]{:S(2)}) collective-permute-start(bf16[1,48,8192]{2,1,0:T(8,128)(2,1)S(1)} %get-tuple-element.10), channel_id=1, source_target_pairs={{0,16},{4,20},{8,24},{12,28},{16,0},{20,4},{24,8},{28,12},{1,17},{... | collective-permute-start | bytes 2359304 | tf_op jit(solution)/shard_map/ppermute | solution.py:19
  34.0 108.4 %collective-permute-start.4 = (bf16[1,48,8192]{2,1,0:T(8,128)(2,1)S(1)}, bf16[1,48,8192]{2,1,0:T(8,128)(2,1)}, u32[]{:S(2)}, u32[]{:S(2)}) collective-permute-start(bf16[1,48,8192]{2,1,0:T(8,128)(2,1)S(1)} %get-tuple-element.9), channel_id=1, source_target_pairs={{0,20},{4,16},{8,28},{12,24},{16,4},{20,0},{24,12},{28,8},{1,21},{... | collective-permute-start | bytes 2359304 | tf_op jit(solution)/shard_map/ppermute | solution.py:19
  38.0 92.9 %all-to-all-start = ((bf16[8,1,48]{2,1,0:T(2,128)(2,1)}), bf16[8,1,48]{2,1,0:T(2,128)(2,1)S(1)}, u32[]{:S(2)}, u32[]{:S(2)}) async-start(bf16[8,1,48]{2,1,0:T(2,128)(2,1)} %convert_element_type.61), calls=%async_computation | async-start | bytes 8192 | tf_op jit(solution)/shard_map/all_to_all | solution.py:60
  43.4 185.2 %all-gather.3.cloned.1.call-start = ((), (), s32[]{:S(2)}) async-start(), calls=%async_computation.1 | async-start | bytes 2359296 | tf_op jit(solution)/shard_map/all_gather | solution.py:31
  131.0 70.6 %collective-permute-start.5 = (bf16[1,48,8192]{2,1,0:T(8,128)(2,1)S(1)}, bf16[1,48,8192]{2,1,0:T(8,128)(2,1)S(1)}, u32[]{:S(2)}, u32[]{:S(2)}) collective-permute-start(bf16[1,48,8192]{2,1,0:T(8,128)(2,1)S(1)} %get-tuple-element.8), channel_id=1, source_target_pairs={{0,24},{4,28},{8,16},{12,20},{16,8},{20,12},{24,0},{28,4},{1,25},{... | collective-permute-start | bytes 2359304 | tf_op jit(solution)/shard_map/ppermute | solution.py:19
  133.7 93.9 %collective-permute-start.6 = (bf16[1,48,8192]{2,1,0:T(8,128)(2,1)S(1)}, bf16[1,48,8192]{2,1,0:T(8,128)(2,1)S(1)}, u32[]{:S(2)}, u32[]{:S(2)}) collective-permute-start(bf16[1,48,8192]{2,1,0:T(8,128)(2,1)S(1)} %get-tuple-element.7), channel_id=1, source_target_pairs={{0,28},{4,24},{8,20},{12,16},{16,12},{20,8},{24,4},{28,0},{1,29},{... | collective-permute-start | bytes 2359304 | tf_op jit(solution)/shard_map/ppermute | solution.py:19
Sparse Core Ops, SparseCore 0:
  130.7 83.0 all-gather.2
